TPU v7x, 32 devices: a whole 2x2x4 slice. The times are simulated.
32 devices in a mesh: area: 4 (over x, core), sub: 8 (over z, y).
Axes of the slice: x: 2, y: 2, z: 4, core: 2. Of those that a mesh axis runs over, the one named last changes fastest.
Arguments:
- blocks: float32 [4, 512, 64, 256], P('area', 'sub'), as said below
- pattern: int32 [4, 512, 4], P('area', 'sub'), may hold values from 0 to 511, as said below
- line_ends: int32 [4, 2, 64], P('area'), may hold values from 0 to 32767, as said below
- sources: float32 [4, 4, 32768], P(None, 'area', 'sub'), may hold values from -6 to 6
- capacity: float32 [4, 32768], P('area', 'sub'), may hold values from 0.2 to 2
- start_volt: float32 [4, 32768], P('area', 'sub'), may hold values from -6 to 6
- start_hist: float32 [4, 2, 64], P('area'), may hold values from -6 to 6
- surge: float32 [4, 64], P('area'), may hold values from 0.2 to 1
Outputs:
- volt: float32 [4, 32768], P('area', 'sub')
- hist: float32 [4, 2, 64], P('area')
Inputs may be any that keep to these rules, and one draw needn't show every extreme that they name: pattern[a, r, 0] = r. Split the 512 block rows of an area into aligned groups of 64: the other entries of a row never point into the row's own group, no two of them in one group are equal, and the entries of one group point into between 27 and 28 distinct block rows of each other group, exactly 28 for some group. `line_ends`: within an area the line-end buses are distinct and rise from the first left end to the last right end. `blocks`: the diagonal of each first stored block lies in 2 to 4.
All inputs are finite; a program needn't handle non-finite values.
Results may differ from a plain program's by a relative error of at most 0.00011.
Values sent between devices are 32-bit elements; how exact they have to be, the bound alone decides.
No kernel may reach another device: no remote copies, remote signals or barrier semaphores. Data moves between devices by JAX's collectives and lax.ppermute only.
A program may use at most 64 MiB of HBM per device.

v0:
```python
import jax
import jax.numpy as jnp
from jax import lax
from jax.sharding import PartitionSpec as P

STEPS = 4
SWEEPS = 8


def shifted(value, axis, steps):
    count = lax.axis_size(axis)
    pairs = [(source, (source + steps) % count) for source in range(count)]
    return lax.ppermute(value, axis, pairs)


def collect(field):
    return lax.all_gather(field, "sub", axis=1, tiled=True)


def apply_blocks(blocks, own_part, others):
    picked = jnp.concatenate([own_part, others], axis=1)
    result = jnp.einsum("rik,rk->ri", blocks[0], picked, precision=lax.Precision.HIGHEST)
    return result.reshape(1, -1)


def on_device(blocks, pattern, line_ends, sources, capacity, start_volt, start_hist, surge):
    width = blocks.shape[2]
    rows_here = blocks.shape[1]
    local_count = rows_here * width
    offset = lax.axis_index("sub") * local_count
    diag = jnp.diagonal(blocks[..., :width], axis1=2, axis2=3).reshape(1, local_count)
    system_diag = diag + capacity
    remote_cols = pattern[0][:, 1:].reshape(-1)
    local_ends = line_ends - offset
    inside = (local_ends >= 0) & (local_ends < local_count)
    safe_ends = jnp.clip(local_ends, 0, local_count - 1)
    volt = start_volt
    hist = start_hist
    carried = []
    for step in range(STEPS):
        rhs = sources[step] + capacity * volt
        inject = jnp.where(inside, -hist, 0.0)
        rhs = rhs.at[0, safe_ends.reshape(-1)].add(inject.reshape(-1))
        field = volt
        for sweep in range(SWEEPS):
            own_part = field.reshape(rows_here, width)
            whole = collect(field)
            others = whole.reshape(-1, width)[remote_cols]
            others = others.reshape(rows_here, -1)
            result = apply_blocks(blocks, own_part, others)
            field = field + (rhs - result - capacity * field) / system_diag
        volt = field
        partial_volt = jnp.where(inside, volt[0][safe_ends[0]][None], 0.0)
        end_volt = lax.psum(partial_volt, "sub")
        message = -2.0 * surge * end_volt[:, 1] - hist[:, 1]
        new_left = shifted(message, "area", 1)
        outgoing_ends = jnp.stack([end_volt[:, 0], hist[:, 0]], axis=1)
        from_right = shifted(outgoing_ends, "area", -1)
        new_right = -2.0 * surge * from_right[:, 0] - from_right[:, 1]
        hist = jnp.stack([new_left, new_right], axis=1)
    return (volt, hist)


def solution(mesh):
    in_specs = (
        P("area", "sub", None, None),
        P("area", "sub", None),
        P("area", None, None),
        P(None, "area", "sub"),
        P("area", "sub"),
        P("area", "sub"),
        P("area", None, None),
        P("area", None),
    )
    out_specs = (P("area", "sub"), P("area", None, None))
    return jax.shard_map(
        on_device, mesh=mesh, in_specs=in_specs, out_specs=out_specs, check_vma=False
    )
```

profile of v0, /device:TPU:0, one launch (start us, length us, event | category | flops | bytes accessed | tf_op | source)
XLA Modules:
  0.0 1362.5 jit_solution(36075500390137617)
XLA Ops:
  2.0 32.5 %all_gather.96 = f32[1,32768]{1,0:T(1,128)S(1)} all-gather(f32[1,4096]{1,0:T(1,128)} %param.13), channel_id=1, replica_groups=mesh['area'=4,'sub'=8] {'sub'}, dimensions={1}, use_global_device_ids=true | all-gather | bytes 147456 | tf_op jit(solution)/shard_map/all_gather | solution.py:17
  51.7 30.5 %all_gather.97 = f32[1,32768]{1,0:T(1,128)S(1)} all-gather(f32[1,4096]{1,0:T(1,128)S(1)} %get-tuple-element.71), channel_id=1, replica_groups=mesh['area'=4,'sub'=8] {'sub'}, dimensions={1}, use_global_device_ids=true | all-gather | bytes 147456 | tf_op jit(solution)/shard_map/all_gather | solution.py:17
  90.7 30.7 %all_gather.98 = f32[1,32768]{1,0:T(1,128)S(1)} all-gather(f32[1,4096]{1,0:T(1,128)S(1)} %get-tuple-element.69), channel_id=1, replica_groups=mesh['area'=4,'sub'=8] {'sub'}, dimensions={1}, use_global_device_ids=true | all-gather | bytes 147456 | tf_op jit(solution)/shard_map/all_gather | solution.py:17
  130.0 30.5 %all_gather.99 = f32[1,32768]{1,0:T(1,128)S(1)} all-gather(f32[1,4096]{1,0:T(1,128)S(1)} %get-tuple-element.67), channel_id=1, replica_groups=mesh['area'=4,'sub'=8] {'sub'}, dimensions={1}, use_global_device_ids=true | all-gather | bytes 147456 | tf_op jit(solution)/shard_map/all_gather | solution.py:17
  169.1 30.5 %all_gather.100 = f32[1,32768]{1,0:T(1,128)S(1)} all-gather(f32[1,4096]{1,0:T(1,128)S(1)} %get-tuple-element.65), channel_id=1, replica_groups=mesh['area'=4,'sub'=8] {'sub'}, dimensions={1}, use_global_device_ids=true | all-gather | bytes 147456 | tf_op jit(solution)/shard_map/all_gather | solution.py:17
  208.2 30.9 %all_gather.101 = f32[1,32768]{1,0:T(1,128)S(1)} all-gather(f32[1,4096]{1,0:T(1,128)S(1)} %get-tuple-element.63), channel_id=1, replica_groups=mesh['area'=4,'sub'=8] {'sub'}, dimensions={1}, use_global_device_ids=true | all-gather | bytes 147456 | tf_op jit(solution)/shard_map/all_gather | solution.py:17
  247.7 30.5 %all_gather.102 = f32[1,32768]{1,0:T(1,128)S(1)} all-gather(f32[1,4096]{1,0:T(1,128)S(1)} %get-tuple-element.61), channel_id=1, replica_groups=mesh['area'=4,'sub'=8] {'sub'}, dimensions={1}, use_global_device_ids=true | all-gather | bytes 147456 | tf_op jit(solution)/shard_map/all_gather | solution.py:17
  286.7 30.5 %all_gather.103 = f32[1,32768]{1,0:T(1,128)S(1)} all-gather(f32[1,4096]{1,0:T(1,128)S(1)} %get-tuple-element.59), channel_id=1, replica_groups=mesh['area'=4,'sub'=8] {'sub'}, dimensions={1}, use_global_device_ids=true | all-gather | bytes 147456 | tf_op jit(solution)/shard_map/all_gather | solution.py:17
  428.7 30.7 %all_gather.106 = f32[1,32768]{1,0:T(1,128)S(1)} all-gather(f32[1,4096]{1,0:T(1,128)S(1)} %get-tuple-element.49), channel_id=1, replica_groups=mesh['area'=4,'sub'=8] {'sub'}, dimensions={1}, use_global_device_ids=true | all-gather | bytes 147456 | tf_op jit(solution)/shard_map/all_gather | solution.py:17
  468.2 30.6 %all_gather.107 = f32[1,32768]{1,0:T(1,128)S(1)} all-gather(f32[1,4096]{1,0:T(1,128)S(1)} %get-tuple-element.47), channel_id=1, replica_groups=mesh['area'=4,'sub'=8] {'sub'}, dimensions={1}, use_global_device_ids=true | all-gather | bytes 147456 | tf_op jit(solution)/shard_map/all_gather | solution.py:17
  507.4 30.6 %all_gather.108 = f32[1,32768]{1,0:T(1,128)S(1)} all-gather(f32[1,4096]{1,0:T(1,128)S(1)} %get-tuple-element.45), channel_id=1, replica_groups=mesh['area'=4,'sub'=8] {'sub'}, dimensions={1}, use_global_device_ids=true | all-gather | bytes 147456 | tf_op jit(solution)/shard_map/all_gather | solution.py:17
  546.7 30.9 %all_gather.109 = f32[1,32768]{1,0:T(1,128)S(1)} all-gather(f32[1,4096]{1,0:T(1,128)S(1)} %get-tuple-element.43), channel_id=1, replica_groups=mesh['area'=4,'sub'=8] {'sub'}, dimensions={1}, use_global_device_ids=true | all-gather | bytes 147456 | tf_op jit(solution)/shard_map/all_gather | solution.py:17
  664.7 30.7 %all_gather.112 = f32[1,32768]{1,0:T(1,128)S(1)} all-gather(f32[1,4096]{1,0:T(1,128)S(1)} %get-tuple-element.35), channel_id=1, replica_groups=mesh['area'=4,'sub'=8] {'sub'}, dimensions={1}, use_global_device_ids=true | all-gather | bytes 147456 | tf_op jit(solution)/shard_map/all_gather | solution.py:17
  726.8 30.6 %all_gather.113 = f32[1,32768]{1,0:T(1,128)S(1)} all-gather(f32[1,4096]{1,0:T(1,128)S(1)} %get-tuple-element.33), channel_id=1, replica_groups=mesh['area'=4,'sub'=8] {'sub'}, dimensions={1}, use_global_device_ids=true | all-gather | bytes 147456 | tf_op jit(solution)/shard_map/all_gather | solution.py:17
  766.1 30.7 %all_gather.114 = f32[1,32768]{1,0:T(1,128)S(1)} all-gather(f32[1,4096]{1,0:T(1,128)S(1)} %get-tuple-element.31), channel_id=1, replica_groups=mesh['area'=4,'sub'=8] {'sub'}, dimensions={1}, use_global_device_ids=true | all-gather | bytes 147456 | tf_op jit(solution)/shard_map/all_gather | solution.py:17
  844.7 30.6 %all_gather.116 = f32[1,32768]{1,0:T(1,128)S(1)} all-gather(f32[1,4096]{1,0:T(1,128)S(1)} %get-tuple-element.27), channel_id=1, replica_groups=mesh['area'=4,'sub'=8] {'sub'}, dimensions={1}, use_global_device_ids=true | all-gather | bytes 147456 | tf_op jit(solution)/shard_map/all_gather | solution.py:17
  884.0 30.9 %all_gather.117 = f32[1,32768]{1,0:T(1,128)S(1)} all-gather(f32[1,4096]{1,0:T(1,128)S(1)} %get-tuple-element.25), channel_id=1, replica_groups=mesh['area'=4,'sub'=8] {'sub'}, dimensions={1}, use_global_device_ids=true | all-gather | bytes 147456 | tf_op jit(solution)/shard_map/all_gather | solution.py:17
  1002.1 30.7 %all_gather.120 = f32[1,32768]{1,0:T(1,128)S(1)} all-gather(f32[1,4096]{1,0:T(1,128)S(1)} %get-tuple-element.17), channel_id=1, replica_groups=mesh['area'=4,'sub'=8] {'sub'}, dimensions={1}, use_global_device_ids=true | all-gather | bytes 147456 | tf_op jit(solution)/shard_map/all_gather | solution.py:17
  1065.2 30.6 %all_gather.121 = f32[1,32768]{1,0:T(1,128)S(1)} all-gather(f32[1,4096]{1,0:T(1,128)S(1)} %get-tuple-element.15), channel_id=1, replica_groups=mesh['area'=4,'sub'=8] {'sub'}, dimensions={1}, use_global_device_ids=true | all-gather | bytes 147456 | tf_op jit(solution)/shard_map/all_gather | solution.py:17
  1104.3 30.8 %all_gather.122 = f32[1,32768]{1,0:T(1,128)S(1)} all-gather(f32[1,4096]{1,0:T(1,128)S(1)} %get-tuple-element.13), channel_id=1, replica_groups=mesh['area'=4,'sub'=8] {'sub'}, dimensions={1}, use_global_device_ids=true | all-gather | bytes 147456 | tf_op jit(solution)/shard_map/all_gather | solution.py:17
  1143.6 30.6 %all_gather.123 = f32[1,32768]{1,0:T(1,128)S(1)} all-gather(f32[1,4096]{1,0:T(1,128)S(1)} %get-tuple-element.11), channel_id=1, replica_groups=mesh['area'=4,'sub'=8] {'sub'}, dimensions={1}, use_global_device_ids=true | all-gather | bytes 147456 | tf_op jit(solution)/shard_map/all_gather | solution.py:17
  1182.8 30.6 %all_gather.124 = f32[1,32768]{1,0:T(1,128)S(1)} all-gather(f32[1,4096]{1,0:T(1,128)S(1)} %get-tuple-element.9), channel_id=1, replica_groups=mesh['area'=4,'sub'=8] {'sub'}, dimensions={1}, use_global_device_ids=true | all-gather | bytes 147456 | tf_op jit(solution)/shard_map/all_gather | solution.py:17
  1221.9 30.8 %all_gather.125 = f32[1,32768]{1,0:T(1,128)S(1)} all-gather(f32[1,4096]{1,0:T(1,128)S(1)} %get-tuple-element.7), channel_id=1, replica_groups=mesh['area'=4,'sub'=8] {'sub'}, dimensions={1}, use_global_device_ids=true | all-gather | bytes 147456 | tf_op jit(solution)/shard_map/all_gather | solution.py:17
  1261.3 30.5 %all_gather.126 = f32[1,32768]{1,0:T(1,128)S(1)} all-gather(f32[1,4096]{1,0:T(1,128)S(1)} %get-tuple-element.5), channel_id=1, replica_groups=mesh['area'=4,'sub'=8] {'sub'}, dimensions={1}, use_global_device_ids=true | all-gather | bytes 147456 | tf_op jit(solution)/shard_map/all_gather | solution.py:17
  (395 shorter events, 622.2 us)
Async XLA Ops:
  37.1 343.3 %copy-start.3 = (s32[1024]{0:T(1024)}, s32[1024]{0:T(1024)S(1)}, u32[]{:S(2)}) copy-start(s32[1024]{0:T(1024)S(1)} %pad_clamp_fusion.1) | copy-start | bytes 12292
  39.4 2.2 copy-start
  39.4 6.1 slice-start
  41.6 9.3 copy-start.2
  41.6 9.3 copy-start.5
  285.9 62.6 %slice-start.1 = ((f32[1,2,64]{2,1,0:T(2,128)}), f32[1,1,64]{2,1,0:T(1,128)S(1)}, s32[]{:S(2)}) async-start(f32[1,2,64]{2,1,0:T(2,128)} %param.14), calls=%async_computation.1 | async-start | bytes 1024 | tf_op jit(solution)/shard_map/slice | solution.py:57
  285.9 93.4 %copy-start.6 = (f32[4,1,4096]{2,1,0:T(1,128)S(1)}, f32[4,1,4096]{2,1,0:T(1,128)}, u32[]{:S(2)}) copy-start(f32[4,1,4096]{2,1,0:T(1,128)} %param.11) | copy-start | bytes 196612
  319.0 62.3 %copy-start.7 = (f32[1,64]{1,0:T(1,128)S(1)}, f32[1,64]{1,0:T(1,128)}, u32[]{:S(2)}) copy-start(f32[1,64]{1,0:T(1,128)} %param.15) | copy-start | bytes 772
  319.0 62.3 %copy-start.8 = (f32[1,2,64]{2,1,0:T(2,128)S(1)}, f32[1,2,64]{2,1,0:T(2,128)}, u32[]{:S(2)}) copy-start(f32[1,2,64]{2,1,0:T(2,128)} %param.14) | copy-start | bytes 1540
  348.5 32.8 %collective-permute-start.1 = (f32[1,2,64]{2,1,0:T(2,128)S(1)}, f32[1,2,64]{2,1,0:T(2,128)S(1)}, u32[]{:S(2)}, u32[]{:S(2)}) collective-permute-start(f32[1,2,64]{2,1,0:T(2,128)S(1)} %pad_maximum_fusion), channel_id=1, source_target_pairs={{0,24},{8,0},{16,8},{24,16},{1,25},{9,1},{17,9},{25,17},{2,26},{10... | collective-permute-start | bytes 1544 | tf_op jit(solution)/shard_map/ppermute | solution.py:13
  381.4 5.9 collective-permute-start
  624.7 71.8 %copy-start.4 = (s32[1024]{0:T(1024)S(1)}, s32[1024]{0:T(1024)}, u32[]{:S(2)}) copy-start(s32[1024]{0:T(1024)} %copy-done.3) | copy-start | bytes 12292
  715.8 1.4 collective-permute-start.3
  717.1 7.4 collective-permute-start.2
  1055.4 1.4 collective-permute-start.5
  1056.8 6.2 collective-permute-start.4
  1338.7 23.3 %copy-start.1 = (f32[1,4096]{1,0:T(1,128)}, f32[1,4096]{1,0:T(1,128)S(1)}, u32[]{:S(2)}) copy-start(f32[1,4096]{1,0:T(1,128)S(1)} %divide_add_fusion) | copy-start | bytes 49156
  1357.1 1.4 collective-permute-start.7
  1358.5 3.0 collective-permute-start.6
where the time goes:
time: 1370 us; the launch traced here: 1360 us
  blocking collectives  1060 us (77%)
  matrix products  181 us (13%)
  other arithmetic  64.7 us (5%)
  local copies, waits for them, and re-layouts  48.1 us (4%)
    all_gather x32, blocking collectives, collect(): return lax.all_gather(field, 'sub', axis=1, tiled=True)  982 us
    dot_general x32, matrix products, apply_blocks(): jnp.einsum('rik,rk->ri', blocks[0], picked, precision=lax.Precision.HIGHEST)  181 us
    psum x4, blocking collectives, on_device(): end_volt = lax.psum(partial_volt, 'sub')  75 us
    all_gather x32, other arithmetic, collect(): return lax.all_gather(field, 'sub', axis=1, tiled=True)  30.4 us
  transfers between devices with their start and end apart: 8, of which 4 were waited for; matrix products, arithmetic and copies ran while one was open for 1% of the time, Pallas kernels for 0%

commit v1 on v0

--- a/solution.py
+++ b/solution.py
@@ -7,6 +7,27 @@
 SWEEPS = 8
 
 
+def collect_2(shard, axis, dim):
+    size, index, span = (lax.axis_size(axis), lax.axis_index(axis), shard.shape[dim])
+    ahead = [(i, (i + 1) % size) for i in range(size)]
+    backward = [(i, (i - 1) % size) for i in range(size)]
+    out = jnp.zeros((*shard.shape[:dim], size * span, *shard.shape[dim + 1 :]), shard.dtype)
+    out = lax.dynamic_update_slice_in_dim(out, shard, index * span, axis=dim)
+    from_left = from_right = shard
+    half = size // 2
+    for turn in range(1, half + 1):
+        from_left = lax.ppermute(from_left, axis, ahead)
+        out = lax.dynamic_update_slice_in_dim(
+            out, from_left, (index - turn) % size * span, axis=dim
+        )
+        if turn < size - half:
+            from_right = lax.ppermute(from_right, axis, backward)
+            out = lax.dynamic_update_slice_in_dim(
+                out, from_right, (index + turn) % size * span, axis=dim
+            )
+    return out
+
+
 def shifted(value, axis, steps):
     count = lax.axis_size(axis)
     pairs = [(source, (source + steps) % count) for source in range(count)]
@@ -14,7 +35,7 @@
 
 
 def collect(field):
-    return lax.all_gather(field, "sub", axis=1, tiled=True)
+    return collect_2(field, "sub", 1)
 
 
 def apply_blocks(blocks, own_part, others):

time: 1370 us -> 1230 us (0.90)
  blocking collectives: 1060 us -> 68.4 us
  starting transfers between devices: 4.31 us -> 462 us
  waiting for transfers between devices: 4.78 us -> 306 us
  local copies, waits for them, and re-layouts: 48.1 us -> 120 us
    all_gather x32 -> x0, blocking collectives: 982 us -> none  [collect(): return lax.all_gather(field, 'sub', axis=1, tiled=True)]
    ppermute x0 -> x224, starting transfers between devices: none -> 461 us  [the longest x96 446 us: collect_2(): from_right = lax.ppermute(from_right, axis, backward)]
    ppermute x0 -> x224, waiting for transfers between devices: none -> 295 us  [the longest x128 295 us: collect_2(): from_left = lax.ppermute(from_left, axis, ahead)]
    dynamic_update_slice x0 -> x253, local copies, waits for them, and re-layouts: none -> 64.5 us  [the longest x129 32.5 us: collect_2(): lax.dynamic_update_slice_in_dim(out, from_left, (index - turn) % size * s...]
    dynamic_update_slice x0 -> x32, other arithmetic: none -> 42.2 us  [collect_2(): lax.dynamic_update_slice_in_dim(out, from_left, (index - turn) % size * s...]
    all_gather x32 -> x0, other arithmetic: 30.4 us -> none  [collect(): return lax.all_gather(field, 'sub', axis=1, tiled=True)]
  transfers between devices with their start and end apart: 8 -> 232, of which waited for: 4 -> 129; matrix products, arithmetic and copies ran while one was open for 1% -> 7% of each run, Pallas kernels for 0% -> 0%
where the time goes in v1:
time: 1230 us; the launch traced here: 1220 us
  starting transfers between devices  462 us (38%)
  waiting for transfers between devices  306 us (25%)
  matrix products  183 us (15%)
  local copies, waits for them, and re-layouts  120 us (10%)
  other arithmetic  76.6 us (6%)
  blocking collectives  68.4 us (6%)
    ppermute x96, starting transfers between devices, collect_2(): from_right = lax.ppermute(from_right, axis, backward)  446 us
    ppermute x128, waiting for transfers between devices, collect_2(): from_left = lax.ppermute(from_left, axis, ahead)  295 us
    dot_general x32, matrix products, apply_blocks(): jnp.einsum('rik,rk->ri', blocks[0], picked, precision=lax.Precision.HIGHEST)  183 us
    psum x4, blocking collectives, on_device(): end_volt = lax.psum(partial_volt, 'sub')  68.4 us
    dynamic_update_slice x32, other arithmetic, collect_2(): lax.dynamic_update_slice_in_dim(out, from_left, (index - turn) % size * s...  42.2 us
    dynamic_update_slice x129, local copies, waits for them, and re-layouts, collect_2(): lax.dynamic_update_slice_in_dim(out, from_left, (index - turn) % size * s...  32.5 us
  transfers between devices with their start and end apart: 232, of which 129 were waited for; matrix products, arithmetic and copies ran while one was open for 7% of the time, Pallas kernels for 0%

profile of v1, /device:TPU:0, one launch (start us, length us, event | category | flops | bytes accessed | tf_op | source)
XLA Modules:
  0.0 1220.7 jit_solution(8632390136626675780)
XLA Ops:
  30.0 6.4 collective-permute-done.6
  64.3 6.4 collective-permute-done.13
  296.9 17.1 %psum.28 = f32[1,2,64]{2,1,0:T(2,128)S(1)} all-reduce(f32[1,2,64]{2,1,0:T(2,128)S(1)} %broadcast_select_fusion.3), channel_id=1, replica_groups=mesh['area'=4,'sub'=8] {'sub'}, use_global_device_ids=true, to_apply=%region_1.2 | all-reduce | flops 128 | bytes 1024 | tf_op jit(solution)/shard_map/psum | solution.py:75
  336.8 6.4 collective-permute-done.64
  605.2 17.1 %psum.29 = f32[1,2,64]{2,1,0:T(2,128)S(1)} all-reduce(f32[1,2,64]{2,1,0:T(2,128)S(1)} %broadcast_select_fusion.2), channel_id=1, replica_groups=mesh['area'=4,'sub'=8] {'sub'}, use_global_device_ids=true, to_apply=%region_3.4 | all-reduce | flops 128 | bytes 1024 | tf_op jit(solution)/shard_map/psum | solution.py:75
  645.0 6.4 collective-permute-done.122
  679.2 6.4 collective-permute-done.129
  713.9 6.4 collective-permute-done.136
  748.1 6.4 collective-permute-done.143
  782.8 6.4 collective-permute-done.150
  817.1 6.4 collective-permute-done.157
  851.7 6.4 collective-permute-done.164
  886.0 6.4 collective-permute-done.171
  902.2 17.1 %psum.30 = f32[1,2,64]{2,1,0:T(2,128)S(1)} all-reduce(f32[1,2,64]{2,1,0:T(2,128)S(1)} %broadcast_select_fusion.1), channel_id=1, replica_groups=mesh['area'=4,'sub'=8] {'sub'}, use_global_device_ids=true, to_apply=%region_5.6 | all-reduce | flops 128 | bytes 1024 | tf_op jit(solution)/shard_map/psum | solution.py:75
  941.9 6.4 collective-permute-done.180
  976.2 6.4 collective-permute-done.187
  1010.9 6.4 collective-permute-done.194
  1045.2 6.4 collective-permute-done.201
  1079.7 6.4 collective-permute-done.208
  1114.0 6.4 collective-permute-done.215
  1148.7 6.4 collective-permute-done.222
  1182.9 6.4 collective-permute-done.229
  1191.3 5.7 fusion
  1198.4 17.1 %psum.31 = f32[1,2,64]{2,1,0:T(2,128)S(1)} all-reduce(f32[1,2,64]{2,1,0:T(2,128)S(1)} %broadcast_select_fusion), channel_id=1, replica_groups=mesh['area'=4,'sub'=8] {'sub'}, use_global_device_ids=true, to_apply=%region_7.8 | all-reduce | flops 128 | bytes 1024 | tf_op jit(solution)/shard_map/psum | solution.py:75
  (1093 shorter events, 1021.6 us)
Async XLA Ops:
  0.6 16.4 %collective-permute-start = (f32[1,4096]{1,0:T(1,128)}, f32[1,4096]{1,0:T(1,128)S(1)}, u32[]{:S(2)}, u32[]{:S(2)}) collective-permute-start(f32[1,4096]{1,0:T(1,128)} %param.13), channel_id=1, source_target_pairs={{0,1},{1,2},{2,3},{3,4},{4,5},{5,6},{6,7},{7,0},{8,9},{9,10},{10,1... | collective-permute-start | bytes 49160 | tf_op jit(solution)/shard_map/ppermute | solution.py:19
  3.7 13.4 %collective-permute-start.1 = (f32[1,4096]{1,0:T(1,128)}, f32[1,4096]{1,0:T(1,128)S(1)}, u32[]{:S(2)}, u32[]{:S(2)}) collective-permute-start(f32[1,4096]{1,0:T(1,128)} %param.13), channel_id=1, source_target_pairs={{0,7},{1,0},{2,1},{3,2},{4,3},{5,4},{6,5},{7,6},{8,15},{9,8},{10,9... | collective-permute-start | bytes 49160 | tf_op jit(solution)/shard_map/ppermute | solution.py:24
  79.3 7.1 collective-permute-start.15
  86.4 6.9 collective-permute-start.17
  92.2 6.9 collective-permute-start.18
  115.7 7.0 collective-permute-start.22
  151.7 7.0 collective-permute-start.29
  187.7 7.0 collective-permute-start.36
  223.7 7.0 collective-permute-start.43
  259.8 7.0 collective-permute-start.50
  314.1 9.4 collective-permute-start.58
  316.1 7.4 collective-permute-start.59
  351.8 7.0 collective-permute-start.66
  387.7 7.0 collective-permute-start.73
  423.8 7.0 collective-permute-start.80
  459.7 7.0 collective-permute-start.87
  495.8 7.0 collective-permute-start.94
  531.7 7.0 collective-permute-start.101
  545.3 6.8 collective-permute-start.105
  568.1 7.0 collective-permute-start.108
  622.4 9.4 collective-permute-start.116
  624.5 7.4 collective-permute-start.117
  919.4 9.4 collective-permute-start.174
  921.4 7.4 collective-permute-start.175
  (218 other events, 1774.5 us)
